TPU v7x, 512 devices: a whole 4x4x16 slice. The times are simulated.
512 devices in a mesh: tm: 128 (over x, z, core), seg: 4 (over y).
Axes of the slice: x: 4, y: 4, z: 16, core: 2. Of those that a mesh axis runs over, the one named last changes fastest.
Arguments:
- samples: float32 [4, 1048576], P('seg', 'tm'), may hold values from -6 to 6
Outputs:
- cyclic: bfloat16 [4, 256, 8, 64, 2, 256], P('seg', 'tm')
All inputs are finite; a program needn't handle non-finite values.
Results may differ from a plain program's by a relative error of at most 0.0084.
Values may be sent and summed in bfloat16 or wider, within the bound.
No kernel may reach another device: no remote copies, remote signals or barrier semaphores. Data moves between devices by JAX's collectives and lax.ppermute only.
A program may use at most 64 MiB of HBM per device.

v0:
```python
import math

import jax
import jax.numpy as jnp
from jax import lax
from jax.sharding import PartitionSpec as P

NP = 256
L2 = 256
Q = 8


def passed_along(value, axis, by):
    length = lax.axis_size(axis)
    return lax.ppermute(value, axis, [(i, (i + by) % length) for i in range(length)])


def shifted(value, axis, steps):
    count = lax.axis_size(axis)
    first, last = (max(0, -steps), min(count, count - steps))
    return lax.ppermute(value, axis, [(source, source + steps) for source in range(first, last)])


def channelize(stream, frame_count, channels):
    hop_len = channels // 4
    rows = stream.reshape(frame_count + 3, hop_len).T
    frames = jnp.concatenate(
        [rows[:, offset : offset + frame_count] for offset in range(4)], axis=0
    )
    sample_pos = jnp.arange(channels, dtype=jnp.int32)
    window = (
        0.5 - 0.5 * jnp.cos(2.0 * math.pi * sample_pos.astype(jnp.float32) / channels)
    ) / math.sqrt(3.0 * channels / 8.0)
    windowed = (frames * window[:, None]).astype(jnp.bfloat16)
    product_idx = sample_pos[:, None] * sample_pos[None, :] % channels
    angles = 2.0 * math.pi * product_idx.astype(jnp.float32) / channels
    dft_table = jnp.concatenate([jnp.cos(angles), -jnp.sin(angles)], axis=0).astype(jnp.bfloat16)
    raw = jnp.dot(dft_table, windowed, preferred_element_type=jnp.float32)
    real_raw = raw[:channels]
    imag_raw = raw[channels:]
    frame_pos = jnp.arange(frame_count, dtype=jnp.int32)
    quarter = sample_pos[:, None] * frame_pos[None, :] % 4
    real_out = jnp.where(
        quarter == 0,
        real_raw,
        jnp.where(quarter == 1, imag_raw, jnp.where(quarter == 2, -real_raw, -imag_raw)),
    )
    imag_out = jnp.where(
        quarter == 0,
        imag_raw,
        jnp.where(quarter == 1, -real_raw, jnp.where(quarter == 2, -imag_raw, real_raw)),
    )
    return jnp.stack([real_out, imag_out]).astype(jnp.bfloat16)


def second_table(length):
    positions = jnp.arange(length, dtype=jnp.int32)
    angles = (
        2.0
        * math.pi
        * (positions[:, None] * positions[None, :] % length).astype(jnp.float32)
        / length
    )
    cosine = jnp.cos(angles) / math.sqrt(length)
    sine = jnp.sin(angles) / math.sqrt(length)
    upper = jnp.stack([cosine, -sine], axis=1)
    lower = jnp.stack([sine, cosine], axis=1)
    return jnp.stack([upper, lower]).astype(jnp.bfloat16)


def pair_products(own_block, partner_block):
    own_real = own_block[0].astype(jnp.float32)
    own_imag = own_block[1].astype(jnp.float32)
    other_real = partner_block[0].astype(jnp.float32)
    other_imag = partner_block[1].astype(jnp.float32)
    return jnp.stack(
        [
            own_real * other_real + own_imag * other_imag,
            own_imag * other_real - own_real * other_imag,
        ]
    ).astype(jnp.bfloat16)


def transform(products, dft_table, length):
    shaped = products.reshape(2, products.shape[1], products.shape[2] // length, length)
    return jnp.einsum("ckbj,cjof->kbof", shaped, dft_table, preferred_element_type=jnp.float32)


def body(samples):
    tm_count = lax.axis_size("tm")
    hop_len = NP // 4
    frame_count = samples.shape[1] // hop_len
    head_rim = samples[:, : 3 * hop_len]
    next_head = passed_along(head_rim, "tm", -1)
    across = shifted(next_head, "seg", -1)
    tail_rim = jnp.where(lax.axis_index("tm") == tm_count - 1, across, next_head)
    stream = jnp.concatenate([samples, tail_rim], axis=1).reshape(-1)
    spectra = channelize(stream, frame_count, NP)
    per_dev = NP // tm_count
    reach_count = (Q - 2 + per_dev) // per_dev
    gathered = lax.all_to_all(spectra, "tm", split_axis=1, concat_axis=2, tiled=True)
    pieces = [gathered]
    for offset in range(1, reach_count + 1):
        pieces.append(passed_along(gathered, "tm", -offset))
    extended = jnp.concatenate(pieces, axis=1)[:, : per_dev + Q - 1]
    own_block = extended[:, :per_dev]
    dft_table = second_table(L2)
    results = []
    for offset in range(Q):
        partner = extended[:, offset : offset + per_dev]
        results.append(
            transform(pair_products(own_block, partner), dft_table, L2).astype(jnp.bfloat16)
        )
    return jnp.stack(results, axis=1)[None]


def solution(mesh):
    return jax.shard_map(
        body,
        mesh=mesh,
        in_specs=(P("seg", "tm"),),
        out_specs=P("seg", "tm", None, None, None, None),
        check_vma=False,
    )
```

profile of v0, /device:TPU:1, one launch (start us, length us, event | category | flops | bytes accessed | tf_op | source)
XLA Modules:
  0.0 75.0 jit_solution(1333757435769018441)
XLA Ops:
  0.0 0.7 slice.129
  0.7 8.7 %collective-permute-start = (f32[1,192]{1,0:T(1,128)S(1)}, f32[1,192]{1,0:T(1,128)S(1)}, u32[]{:S(2)}, u32[]{:S(2)}) collective-permute-start(f32[1,192]{1,0:T(1,128)S(1)} %slice.129), channel_id=1, source_target_pairs={{0,508},{4,0},{8,4},{12,8},{16,12},{20,16},{24,20},{28,24},{32,28}... | collective-permute-start | bytes 2312 | tf_op jit(solution)/shard_map/ppermute | solution.py:15
  9.4 1.1 %negate_convert_fusion.1 = (bf16[256,256]{1,0:T(8,128)(2,1)S(1)}, bf16[256,256]{1,0:T(8,128)(2,1)S(1)}) fusion(), kind=kLoop, calls=%fused_computation.56 | loop fusion | flops 1114112 | bytes 262144 | tf_op jit(solution)/shard_map/convert.47
  10.6 1.3 %collective-permute-start.1 = (f32[1,192]{1,0:T(1,128)S(1)}, f32[1,192]{1,0:T(1,128)S(1)}, u32[]{:S(2)}, u32[]{:S(2)}) collective-permute-start(f32[1,192]{1,0:T(1,128)S(1)} %collective-permute-done), channel_id=1, source_target_pairs={{1,0},{2,1},{3,2},{5,4},{6,5},{7,6},{9,8},{10,9},{11,10},{13,12},{... | collective-permute-start | bytes 2312 | tf_op jit(solution)/shard_map/ppermute | solution.py:21
  11.9 3.0 %collective-permute-done.1 = f32[1,192]{1,0:T(1,128)S(1)} collective-permute-done((f32[1,192]{1,0:T(1,128)S(1)}, f32[1,192]{1,0:T(1,128)S(1)}, u32[]{:S(2)}, u32[]{:S(2)}) %collective-permute-start.1) | collective-permute-done | bytes 800 | tf_op jit(solution)/shard_map/ppermute | solution.py:21
  15.1 0.3 fusion.30
  15.5 0.8 %copy.10 = bf16[2,256,128]{2,0,1:T(2,128)(2,1)} copy(bf16[2,256,128]{2,1,0:T(8,128)(2,1)S(1)} %pad_maximum_fusion) | data formatting | bytes 262144 | tf_op jit(solution)/shard_map/stack | solution.py:53
  16.3 14.9 %all-to-all-start = ((bf16[2,256,128]{2,0,1:T(2,128)(2,1)}), bf16[2,256,128]{2,0,1:T(2,128)(2,1)S(1)}, u32[]{:S(2)}, u32[]{:S(2)}) async-start(bf16[2,256,128]{2,0,1:T(2,128)(2,1)} %copy.10), calls=%async_computation | async-start | bytes 262144 | tf_op jit(solution)/shard_map/all_to_all | solution.py:101
  31.2 1.0 %fusion.40 = bf16[256,1,256]{2,0,1:T(8,128)(2,1)S(1)} fusion(), kind=kLoop, calls=%fused_computation.62 | loop fusion | flops 1048576 | bytes 131072 | tf_op jit(solution)/shard_map/convert.33
  32.2 1.1 %negate_convert_fusion = (bf16[256,1,256]{2,0,1:T(8,128)(2,1)S(1)}, bf16[256,1,256]{2,0,1:T(8,128)(2,1)S(1)}) fusion(), kind=kLoop, calls=%fused_computation.51 | loop fusion | flops 1245184 | bytes 262144 | tf_op jit(solution)/shard_map/convert.37
  33.3 15.1 %all-to-all-done = bf16[2,256,128]{2,0,1:T(2,128)(2,1)S(1)} async-done(((bf16[2,256,128]{2,0,1:T(2,128)(2,1)}), bf16[2,256,128]{2,0,1:T(2,128)(2,1)S(1)}, u32[]{:S(2)}, u32[]{:S(2)}) %all-to-all-start) | async-done | bytes 131104 | tf_op jit(solution)/shard_map/all_to_all | solution.py:101
  48.6 3.7 %collective-permute-start.3 = (bf16[2,2,16384]{2,1,0:T(2,128)(2,1)S(1)}, bf16[2,2,16384]{2,1,0:T(2,128)(2,1)S(1)}, u32[]{:S(2)}, u32[]{:S(2)}) collective-permute-start(bf16[2,2,16384]{2,1,0:T(2,128)(2,1)S(1)} %all_to_all.16), channel_id=1, source_target_pairs={{0,504},{4,508},{8,0},{12,4},{16,8},{20,12},{24,16},{28,20},{32,24... | collective-permute-start | bytes 393224 | tf_op jit(solution)/shard_map/ppermute | solution.py:15
  52.3 2.6 %collective-permute-start.2 = (bf16[2,2,16384]{2,1,0:T(2,128)(2,1)S(1)}, bf16[2,2,16384]{2,1,0:T(2,128)(2,1)S(1)}, u32[]{:S(2)}, u32[]{:S(2)}) collective-permute-start(bf16[2,2,16384]{2,1,0:T(2,128)(2,1)S(1)} %all_to_all.16), channel_id=1, source_target_pairs={{0,508},{4,0},{8,4},{12,8},{16,12},{20,16},{24,20},{28,24},{32,28}... | collective-permute-start | bytes 393224 | tf_op jit(solution)/shard_map/ppermute | solution.py:15
  55.0 2.4 %collective-permute-start.5 = (bf16[2,2,16384]{2,1,0:T(2,128)(2,1)S(1)}, bf16[2,2,16384]{2,1,0:T(2,128)(2,1)S(1)}, u32[]{:S(2)}, u32[]{:S(2)}) collective-permute-start(bf16[2,2,16384]{2,1,0:T(2,128)(2,1)S(1)} %all_to_all.16), channel_id=1, source_target_pairs={{0,496},{4,500},{8,504},{12,508},{16,0},{20,4},{24,8},{28,12},{32,... | collective-permute-start | bytes 393224 | tf_op jit(solution)/shard_map/ppermute | solution.py:15
  57.4 2.6 %collective-permute-start.4 = (bf16[2,2,16384]{2,1,0:T(2,128)(2,1)S(1)}, bf16[2,2,16384]{2,1,0:T(2,128)(2,1)S(1)}, u32[]{:S(2)}, u32[]{:S(2)}) collective-permute-start(bf16[2,2,16384]{2,1,0:T(2,128)(2,1)S(1)} %all_to_all.16), channel_id=1, source_target_pairs={{0,500},{4,504},{8,508},{12,0},{16,4},{20,8},{24,12},{28,16},{32,2... | collective-permute-start | bytes 393224 | tf_op jit(solution)/shard_map/ppermute | solution.py:15
  60.5 0.9 %fusion.50 = (bf16[1,2,16384]{2,1,0:T(2,128)(2,1)S(1)}, bf16[1,2,16384]{2,1,0:T(2,128)(2,1)S(1)}, bf16[1,2,16384]{2,1,0:T(2,128)(2,1)S(1)}, bf16[1,2,16384]{2,1,...) fusion(f32[1,2,16384]{2,1,0:T(2,128)S(1)} %reshape.217, ...), kind=kLoop, calls=%fused_computation.103 | loop fusion | flops 1245184 | bytes 1310720 | tf_op jit(solution)/shard_map/convert.21
  61.5 2.8 %collective-permute-done.5 = bf16[2,2,16384]{2,1,0:T(2,128)(2,1)S(1)} collective-permute-done((bf16[2,2,16384]{2,1,0:T(2,128)(2,1)S(1)}, bf16[2,2,16384]{2,1,0:T(2,128)(2,1)S(1)}, u32[]{:S(2)}, u32[]{:S(2)}) %collective-permute-start.5) | collective-permute-done | bytes 131104 | tf_op jit(solution)/shard_map/ppermute | solution.py:15
  64.3 5.2 %collective-permute-done.4 = bf16[2,2,16384]{2,1,0:T(2,128)(2,1)S(1)} collective-permute-done((bf16[2,2,16384]{2,1,0:T(2,128)(2,1)S(1)}, bf16[2,2,16384]{2,1,0:T(2,128)(2,1)S(1)}, u32[]{:S(2)}, u32[]{:S(2)}) %collective-permute-start.4) | collective-permute-done | bytes 131104 | tf_op jit(solution)/shard_map/ppermute | solution.py:15
  69.4 1.1 %fusion.66 = (bf16[1,2,16384]{2,1,0:T(2,128)(2,1)S(1)}, bf16[1,2,16384]{2,1,0:T(2,128)(2,1)S(1)}, bf16[1,2,16384]{2,1,0:T(2,128)(2,1)S(1)}, bf16[1,2,16384]{2,1,...) fusion(f32[1,2,16384]{2,1,0:T(2,128)S(1)} %reshape.217, ...), kind=kLoop, calls=%fused_computation.119 | loop fusion | flops 1572864 | bytes 1572864 | tf_op jit(solution)/shard_map/convert.5
  70.6 0.4 fusion.68
  72.2 0.2 fusion.13
  72.4 0.2 fusion.11
  72.7 0.2 fusion.9
  72.9 2.1 %copy.13 = bf16[1,2,8,64,2,256]{5,4,3,2,1,0:T(2,128)(2,1)} copy(bf16[1,2,8,64,2,256]{5,3,4,1,2,0:T(8,128)(2,1)S(1)} %bitcast.282) | data formatting | bytes 2097152 | tf_op jit(solution)/shard_map/broadcast_in_dim | solution.py:114
  (40 shorter events, 2.1 us)
Async XLA Ops:
  0.7 9.9 %collective-permute-start = (f32[1,192]{1,0:T(1,128)S(1)}, f32[1,192]{1,0:T(1,128)S(1)}, u32[]{:S(2)}, u32[]{:S(2)}) collective-permute-start(f32[1,192]{1,0:T(1,128)S(1)} %slice.129), channel_id=1, source_target_pairs={{0,508},{4,0},{8,4},{12,8},{16,12},{20,16},{24,20},{28,24},{32,28}... | collective-permute-start | bytes 2312 | tf_op jit(solution)/shard_map/ppermute | solution.py:15
  9.4 5.5 %copy-start = (f32[1,8192]{1,0:T(1,128)S(1)}, f32[1,8192]{1,0:T(1,128)}, u32[]{:S(2)}) copy-start(f32[1,8192]{1,0:T(1,128)} %param.1) | copy-start | bytes 98308
  10.6 4.3 %collective-permute-start.1 = (f32[1,192]{1,0:T(1,128)S(1)}, f32[1,192]{1,0:T(1,128)S(1)}, u32[]{:S(2)}, u32[]{:S(2)}) collective-permute-start(f32[1,192]{1,0:T(1,128)S(1)} %collective-permute-done), channel_id=1, source_target_pairs={{1,0},{2,1},{3,2},{5,4},{6,5},{7,6},{9,8},{10,9},{11,10},{13,12},{... | collective-permute-start | bytes 2312 | tf_op jit(solution)/shard_map/ppermute | solution.py:21
  16.3 32.2 %all-to-all-start = ((bf16[2,256,128]{2,0,1:T(2,128)(2,1)}), bf16[2,256,128]{2,0,1:T(2,128)(2,1)S(1)}, u32[]{:S(2)}, u32[]{:S(2)}) async-start(bf16[2,256,128]{2,0,1:T(2,128)(2,1)} %copy.10), calls=%async_computation | async-start | bytes 262144 | tf_op jit(solution)/shard_map/all_to_all | solution.py:101
  48.6 11.9 %collective-permute-start.3 = (bf16[2,2,16384]{2,1,0:T(2,128)(2,1)S(1)}, bf16[2,2,16384]{2,1,0:T(2,128)(2,1)S(1)}, u32[]{:S(2)}, u32[]{:S(2)}) collective-permute-start(bf16[2,2,16384]{2,1,0:T(2,128)(2,1)S(1)} %all_to_all.16), channel_id=1, source_target_pairs={{0,504},{4,508},{8,0},{12,4},{16,8},{20,12},{24,16},{28,20},{32,24... | collective-permute-start | bytes 393224 | tf_op jit(solution)/shard_map/ppermute | solution.py:15
  52.3 8.2 %collective-permute-start.2 = (bf16[2,2,16384]{2,1,0:T(2,128)(2,1)S(1)}, bf16[2,2,16384]{2,1,0:T(2,128)(2,1)S(1)}, u32[]{:S(2)}, u32[]{:S(2)}) collective-permute-start(bf16[2,2,16384]{2,1,0:T(2,128)(2,1)S(1)} %all_to_all.16), channel_id=1, source_target_pairs={{0,508},{4,0},{8,4},{12,8},{16,12},{20,16},{24,20},{28,24},{32,28}... | collective-permute-start | bytes 393224 | tf_op jit(solution)/shard_map/ppermute | solution.py:15
  55.0 9.3 %collective-permute-start.5 = (bf16[2,2,16384]{2,1,0:T(2,128)(2,1)S(1)}, bf16[2,2,16384]{2,1,0:T(2,128)(2,1)S(1)}, u32[]{:S(2)}, u32[]{:S(2)}) collective-permute-start(bf16[2,2,16384]{2,1,0:T(2,128)(2,1)S(1)} %all_to_all.16), channel_id=1, source_target_pairs={{0,496},{4,500},{8,504},{12,508},{16,0},{20,4},{24,8},{28,12},{32,... | collective-permute-start | bytes 393224 | tf_op jit(solution)/shard_map/ppermute | solution.py:15
  57.4 12.1 %collective-permute-start.4 = (bf16[2,2,16384]{2,1,0:T(2,128)(2,1)S(1)}, bf16[2,2,16384]{2,1,0:T(2,128)(2,1)S(1)}, u32[]{:S(2)}, u32[]{:S(2)}) collective-permute-start(bf16[2,2,16384]{2,1,0:T(2,128)(2,1)S(1)} %all_to_all.16), channel_id=1, source_target_pairs={{0,500},{4,504},{8,508},{12,0},{16,4},{20,8},{24,12},{28,16},{32,2... | collective-permute-start | bytes 393224 | tf_op jit(solution)/shard_map/ppermute | solution.py:15
where the time goes:
time: 75.3 us; the launch traced here: 75 us
  starting transfers between devices  36.2 us (48%)
  waiting for transfers between devices  26.1 us (35%)
  other arithmetic  6.06 us (8%)
  local copies, waits for them, and re-layouts  4.04 us (5%)
  matrix products  2.19 us (3%)
    ppermute x5, starting transfers between devices, passed_along(): lax.ppermute(value, axis, [(i, (i + by) % length) for i in range(length)])  20.1 us
    all_to_all x1, waiting for transfers between devices, body(): lax.all_to_all(spectra, 'tm', split_axis=1, concat_axis=2, tiled=True)  15.1 us
    all_to_all x1, starting transfers between devices, body(): lax.all_to_all(spectra, 'tm', split_axis=1, concat_axis=2, tiled=True)  14.9 us
    ppermute x5, waiting for transfers between devices, passed_along(): lax.ppermute(value, axis, [(i, (i + by) % length) for i in range(length)])  7.95 us
    another operation x7, other arithmetic  5.72 us
    ppermute x1, waiting for transfers between devices, shifted(): lax.ppermute(value, axis, [(source, source + steps) for source in range(f...  2.97 us
    broadcast_in_dim x1, local copies, waits for them, and re-layouts, body(): return jnp.stack(results, axis=1)[None]  2.06 us
    dot_general x8, matrix products, transform(): jnp.einsum('ckbj,cjof->kbof', shaped, dft_table, preferred_element_type=j...  1.89 us
  transfers between devices with their start and end apart: 7, of which 4 were waited for; matrix products, arithmetic and copies ran while one was open for 6% of the time, Pallas kernels for 0%

commit v1 on v0

--- a/solution.py
+++ b/solution.py
@@ -13,12 +13,6 @@
 def passed_along(value, axis, by):
     length = lax.axis_size(axis)
     return lax.ppermute(value, axis, [(i, (i + by) % length) for i in range(length)])
-
-
-def shifted(value, axis, steps):
-    count = lax.axis_size(axis)
-    first, last = (max(0, -steps), min(count, count - steps))
-    return lax.ppermute(value, axis, [(source, source + steps) for source in range(first, last)])
 
 
 def channelize(stream, frame_count, channels):
@@ -88,21 +82,29 @@
 
 def body(samples):
     tm_count = lax.axis_size("tm")
+    seg_count = lax.axis_size("seg")
     hop_len = NP // 4
     frame_count = samples.shape[1] // hop_len
     head_rim = samples[:, : 3 * hop_len]
-    next_head = passed_along(head_rim, "tm", -1)
-    across = shifted(next_head, "seg", -1)
-    tail_rim = jnp.where(lax.axis_index("tm") == tm_count - 1, across, next_head)
+    def flat(s, t):
+        return t * seg_count + s
+
+    pairs = [(flat(s, t), flat(s, t - 1)) for s in range(seg_count) for t in range(1, tm_count)]
+    pairs += [(flat(s + 1, 0), flat(s, tm_count - 1)) for s in range(seg_count - 1)]
+    tail_rim = lax.ppermute(head_rim, ("tm", "seg"), pairs)
     stream = jnp.concatenate([samples, tail_rim], axis=1).reshape(-1)
     spectra = channelize(stream, frame_count, NP)
     per_dev = NP // tm_count
-    reach_count = (Q - 2 + per_dev) // per_dev
     gathered = lax.all_to_all(spectra, "tm", split_axis=1, concat_axis=2, tiled=True)
     pieces = [gathered]
-    for offset in range(1, reach_count + 1):
-        pieces.append(passed_along(gathered, "tm", -offset))
-    extended = jnp.concatenate(pieces, axis=1)[:, : per_dev + Q - 1]
+    need = Q - 1
+    offset = 1
+    while need > 0:
+        take = min(per_dev, need)
+        pieces.append(passed_along(gathered[:, :take], "tm", -offset))
+        need -= take
+        offset += 1
+    extended = jnp.concatenate(pieces, axis=1)
     own_block = extended[:, :per_dev]
     dft_table = second_table(L2)
     results = []

time: 75.3 us -> 71.1 us (0.944)
  waiting for transfers between devices: 26.1 us -> 23.4 us
  starting transfers between devices: 36.2 us -> 34.7 us
    ppermute x5 -> x4, starting transfers between devices: 20.1 us -> 11.1 us  [passed_along(): lax.ppermute(value, axis, [(i, (i + by) % length) for i in range(length)])]
    ppermute x1, starting transfers between devices: 1.29 us -> 8.87 us  [body(): tail_rim = lax.ppermute(head_rim, ('tm', 'seg'), pairs)]
    ppermute x1, waiting for transfers between devices: 2.97 us -> 0.01 us  [body(): tail_rim = lax.ppermute(head_rim, ('tm', 'seg'), pairs)]
    ppermute x5 -> x4, waiting for transfers between devices: 7.95 us -> 8.28 us  [passed_along(): lax.ppermute(value, axis, [(i, (i + by) % length) for i in range(length)])]
  transfers between devices with their start and end apart: 7 -> 6, of which waited for: 4 -> 2; matrix products, arithmetic and copies ran while one was open for 6% -> 7% of each run, Pallas kernels for 0% -> 0%
where the time goes in v1:
time: 71.1 us; the launch traced here: 70.8 us
  starting transfers between devices  34.7 us (49%)
  waiting for transfers between devices  23.4 us (33%)
  other arithmetic  6.05 us (9%)
  local copies, waits for them, and re-layouts  4.03 us (6%)
  matrix products  2.18 us (3%)
    all_to_all x1, waiting for transfers between devices, body(): lax.all_to_all(spectra, 'tm', split_axis=1, concat_axis=2, tiled=True)  15.1 us
    all_to_all x1, starting transfers between devices, body(): lax.all_to_all(spectra, 'tm', split_axis=1, concat_axis=2, tiled=True)  14.8 us
    ppermute x4, starting transfers between devices, passed_along(): lax.ppermute(value, axis, [(i, (i + by) % length) for i in range(length)])  11.1 us
    ppermute x1, starting transfers between devices, body(): tail_rim = lax.ppermute(head_rim, ('tm', 'seg'), pairs)  8.87 us
    ppermute x4, waiting for transfers between devices, passed_along(): lax.ppermute(value, axis, [(i, (i + by) % length) for i in range(length)])  8.28 us
    another operation x7, other arithmetic  5.72 us
    broadcast_in_dim x1, local copies, waits for them, and re-layouts, body(): return jnp.stack(results, axis=1)[None]  2.06 us
    dot_general x8, matrix products, transform(): jnp.einsum('ckbj,cjof->kbof', shaped, dft_table, preferred_element_type=j...  1.88 us
  transfers between devices with their start and end apart: 6, of which 2 were waited for; matrix products, arithmetic and copies ran while one was open for 7% of the time, Pallas kernels for 0%

profile of v1, /device:TPU:1, one launch (start us, length us, event | category | flops | bytes accessed | tf_op | source)
XLA Modules:
  0.0 70.8 jit_solution(10910522550809654180)
XLA Ops:
  0.0 0.7 slice.106
  0.7 8.9 %collective-permute-start = (f32[1,192]{1,0:T(1,128)S(1)}, f32[1,192]{1,0:T(1,128)S(1)}, u32[]{:S(2)}, u32[]{:S(2)}) collective-permute-start(f32[1,192]{1,0:T(1,128)S(1)} %slice.106), channel_id=1, source_target_pairs={{4,0},{8,4},{12,8},{16,12},{20,16},{24,20},{28,24},{32,28},{36,32}... | collective-permute-start | bytes 2312 | tf_op jit(solution)/shard_map/ppermute | solution.py:94
  9.6 1.1 %negate_convert_fusion.1 = (bf16[256,256]{1,0:T(8,128)(2,1)S(1)}, bf16[256,256]{1,0:T(8,128)(2,1)S(1)}) fusion(), kind=kLoop, calls=%fused_computation.56 | loop fusion | flops 1114112 | bytes 262144 | tf_op jit(solution)/shard_map/convert.47
  10.9 0.3 fusion.30
  11.4 0.8 %copy.10 = bf16[2,256,128]{2,0,1:T(2,128)(2,1)} copy(bf16[2,256,128]{2,1,0:T(8,128)(2,1)S(1)} %pad_maximum_fusion) | data formatting | bytes 262144 | tf_op jit(solution)/shard_map/stack | solution.py:47
  12.2 14.8 %all-to-all-start = ((bf16[2,256,128]{2,0,1:T(2,128)(2,1)}), bf16[2,256,128]{2,0,1:T(2,128)(2,1)S(1)}, u32[]{:S(2)}, u32[]{:S(2)}) async-start(bf16[2,256,128]{2,0,1:T(2,128)(2,1)} %copy.10), calls=%async_computation | async-start | bytes 262144 | tf_op jit(solution)/shard_map/all_to_all | solution.py:98
  27.0 1.0 %fusion.40 = bf16[256,1,256]{2,0,1:T(8,128)(2,1)S(1)} fusion(), kind=kLoop, calls=%fused_computation.62 | loop fusion | flops 1048576 | bytes 131072 | tf_op jit(solution)/shard_map/convert.33
  28.0 1.1 %negate_convert_fusion = (bf16[256,1,256]{2,0,1:T(8,128)(2,1)S(1)}, bf16[256,1,256]{2,0,1:T(8,128)(2,1)S(1)}) fusion(), kind=kLoop, calls=%fused_computation.51 | loop fusion | flops 1245184 | bytes 262144 | tf_op jit(solution)/shard_map/convert.37
  29.1 15.1 %all-to-all-done = bf16[2,256,128]{2,0,1:T(2,128)(2,1)S(1)} async-done(((bf16[2,256,128]{2,0,1:T(2,128)(2,1)}), bf16[2,256,128]{2,0,1:T(2,128)(2,1)S(1)}, u32[]{:S(2)}, u32[]{:S(2)}) %all-to-all-start) | async-done | bytes 131104 | tf_op jit(solution)/shard_map/all_to_all | solution.py:98
  44.4 3.7 %collective-permute-start.2 = (bf16[2,2,16384]{2,1,0:T(2,128)(2,1)S(1)}, bf16[2,2,16384]{2,1,0:T(2,128)(2,1)S(1)}, u32[]{:S(2)}, u32[]{:S(2)}) collective-permute-start(bf16[2,2,16384]{2,1,0:T(2,128)(2,1)S(1)} %all_to_all.16), channel_id=1, source_target_pairs={{0,504},{4,508},{8,0},{12,4},{16,8},{20,12},{24,16},{28,20},{32,24... | collective-permute-start | bytes 393224 | tf_op jit(solution)/shard_map/ppermute | solution.py:15
  48.1 2.6 %collective-permute-start.1 = (bf16[2,2,16384]{2,1,0:T(2,128)(2,1)S(1)}, bf16[2,2,16384]{2,1,0:T(2,128)(2,1)S(1)}, u32[]{:S(2)}, u32[]{:S(2)}) collective-permute-start(bf16[2,2,16384]{2,1,0:T(2,128)(2,1)S(1)} %all_to_all.16), channel_id=1, source_target_pairs={{0,508},{4,0},{8,4},{12,8},{16,12},{20,16},{24,20},{28,24},{32,28}... | collective-permute-start | bytes 393224 | tf_op jit(solution)/shard_map/ppermute | solution.py:15
  50.8 2.7 %collective-permute-start.3 = (bf16[2,2,16384]{2,1,0:T(2,128)(2,1)S(1)}, bf16[2,2,16384]{2,1,0:T(2,128)(2,1)S(1)}, u32[]{:S(2)}, u32[]{:S(2)}) collective-permute-start(bf16[2,2,16384]{2,1,0:T(2,128)(2,1)S(1)} %all_to_all.16), channel_id=1, source_target_pairs={{0,500},{4,504},{8,508},{12,0},{16,4},{20,8},{24,12},{28,16},{32,2... | collective-permute-start | bytes 393224 | tf_op jit(solution)/shard_map/ppermute | solution.py:15
  53.7 2.1 %collective-permute-start.4 = (bf16[2,1,16384]{2,1,0:T(2,128)(2,1)S(1)}, bf16[2,1,16384]{2,1,0:T(2,128)(2,1)S(1)}, u32[]{:S(2)}, u32[]{:S(2)}) collective-permute-start(bf16[2,1,16384]{2,1,0:T(2,128)(2,1)S(1)} %bitcast.284), channel_id=1, source_target_pairs={{0,496},{4,500},{8,504},{12,508},{16,0},{20,4},{24,8},{28,12},{32,... | collective-permute-start | bytes 196616 | tf_op jit(solution)/shard_map/ppermute | solution.py:15
  55.8 0.2 fusion.23
  56.0 0.9 %fusion.50 = (bf16[1,2,16384]{2,1,0:T(2,128)(2,1)S(1)}, bf16[1,2,16384]{2,1,0:T(2,128)(2,1)S(1)}, bf16[1,2,16384]{2,1,0:T(2,128)(2,1)S(1)}, bf16[1,2,16384]{2,1,...) fusion(f32[1,2,16384]{2,1,0:T(2,128)S(1)} %reshape.234, ...), kind=kLoop, calls=%fused_computation.103 | loop fusion | flops 1245184 | bytes 1310720 | tf_op jit(solution)/shard_map/convert.21
  57.0 8.3 %collective-permute-done.4 = bf16[2,1,16384]{2,1,0:T(2,128)(2,1)S(1)} collective-permute-done((bf16[2,1,16384]{2,1,0:T(2,128)(2,1)S(1)}, bf16[2,1,16384]{2,1,0:T(2,128)(2,1)S(1)}, u32[]{:S(2)}, u32[]{:S(2)}) %collective-permute-start.4) | collective-permute-done | bytes 65568 | tf_op jit(solution)/shard_map/ppermute | solution.py:15
  65.3 1.1 %fusion.66 = (bf16[1,2,16384]{2,1,0:T(2,128)(2,1)S(1)}, bf16[1,2,16384]{2,1,0:T(2,128)(2,1)S(1)}, bf16[1,2,16384]{2,1,0:T(2,128)(2,1)S(1)}, bf16[1,2,16384]{2,1,...) fusion(f32[1,2,16384]{2,1,0:T(2,128)S(1)} %reshape.234, ...), kind=kLoop, calls=%fused_computation.119 | loop fusion | flops 1572864 | bytes 1572864 | tf_op jit(solution)/shard_map/convert.5
  66.5 0.4 fusion.68
  67.0 0.2 fusion.21
  67.3 0.2 fusion.19
  67.5 0.2 fusion.17
  67.8 0.2 fusion.15
  68.5 0.2 fusion.9
  68.7 2.1 %copy.13 = bf16[1,2,8,64,2,256]{5,4,3,2,1,0:T(2,128)(2,1)} copy(bf16[1,2,8,64,2,256]{5,3,4,1,2,0:T(8,128)(2,1)S(1)} %bitcast.283) | data formatting | bytes 2097152 | tf_op jit(solution)/shard_map/broadcast_in_dim | solution.py:116
  (37 shorter events, 1.4 us)
Async XLA Ops:
  0.7 10.0 %copy-start = (f32[1,8192]{1,0:T(1,128)S(1)}, f32[1,8192]{1,0:T(1,128)}, u32[]{:S(2)}) copy-start(f32[1,8192]{1,0:T(1,128)} %param.1) | copy-start | bytes 98308
  0.7 10.0 %collective-permute-start = (f32[1,192]{1,0:T(1,128)S(1)}, f32[1,192]{1,0:T(1,128)S(1)}, u32[]{:S(2)}, u32[]{:S(2)}) collective-permute-start(f32[1,192]{1,0:T(1,128)S(1)} %slice.106), channel_id=1, source_target_pairs={{4,0},{8,4},{12,8},{16,12},{20,16},{24,20},{28,24},{32,28},{36,32}... | collective-permute-start | bytes 2312 | tf_op jit(solution)/shard_map/ppermute | solution.py:94
  12.2 32.1 %all-to-all-start = ((bf16[2,256,128]{2,0,1:T(2,128)(2,1)}), bf16[2,256,128]{2,0,1:T(2,128)(2,1)S(1)}, u32[]{:S(2)}, u32[]{:S(2)}) async-start(bf16[2,256,128]{2,0,1:T(2,128)(2,1)} %copy.10), calls=%async_computation | async-start | bytes 262144 | tf_op jit(solution)/shard_map/all_to_all | solution.py:98
  44.4 11.6 %collective-permute-start.2 = (bf16[2,2,16384]{2,1,0:T(2,128)(2,1)S(1)}, bf16[2,2,16384]{2,1,0:T(2,128)(2,1)S(1)}, u32[]{:S(2)}, u32[]{:S(2)}) collective-permute-start(bf16[2,2,16384]{2,1,0:T(2,128)(2,1)S(1)} %all_to_all.16), channel_id=1, source_target_pairs={{0,504},{4,508},{8,0},{12,4},{16,8},{20,12},{24,16},{28,20},{32,24... | collective-permute-start | bytes 393224 | tf_op jit(solution)/shard_map/ppermute | solution.py:15
  48.1 7.9 %collective-permute-start.1 = (bf16[2,2,16384]{2,1,0:T(2,128)(2,1)S(1)}, bf16[2,2,16384]{2,1,0:T(2,128)(2,1)S(1)}, u32[]{:S(2)}, u32[]{:S(2)}) collective-permute-start(bf16[2,2,16384]{2,1,0:T(2,128)(2,1)S(1)} %all_to_all.16), channel_id=1, source_target_pairs={{0,508},{4,0},{8,4},{12,8},{16,12},{20,16},{24,20},{28,24},{32,28}... | collective-permute-start | bytes 393224 | tf_op jit(solution)/shard_map/ppermute | solution.py:15
  50.8 14.5 %collective-permute-start.3 = (bf16[2,2,16384]{2,1,0:T(2,128)(2,1)S(1)}, bf16[2,2,16384]{2,1,0:T(2,128)(2,1)S(1)}, u32[]{:S(2)}, u32[]{:S(2)}) collective-permute-start(bf16[2,2,16384]{2,1,0:T(2,128)(2,1)S(1)} %all_to_all.16), channel_id=1, source_target_pairs={{0,500},{4,504},{8,508},{12,0},{16,4},{20,8},{24,12},{28,16},{32,2... | collective-permute-start | bytes 393224 | tf_op jit(solution)/shard_map/ppermute | solution.py:15
  53.7 11.6 %collective-permute-start.4 = (bf16[2,1,16384]{2,1,0:T(2,128)(2,1)S(1)}, bf16[2,1,16384]{2,1,0:T(2,128)(2,1)S(1)}, u32[]{:S(2)}, u32[]{:S(2)}) collective-permute-start(bf16[2,1,16384]{2,1,0:T(2,128)(2,1)S(1)} %bitcast.284), channel_id=1, source_target_pairs={{0,496},{4,500},{8,504},{12,508},{16,0},{20,4},{24,8},{28,12},{32,... | collective-permute-start | bytes 196616 | tf_op jit(solution)/shard_map/ppermute | solution.py:15

commit v2 on v1

--- a/solution.py
+++ b/solution.py
@@ -1,6 +1,7 @@
 import math
 
 import jax
+import numpy as np
 import jax.numpy as jnp
 from jax import lax
 from jax.sharding import PartitionSpec as P
@@ -26,9 +27,7 @@
         0.5 - 0.5 * jnp.cos(2.0 * math.pi * sample_pos.astype(jnp.float32) / channels)
     ) / math.sqrt(3.0 * channels / 8.0)
     windowed = (frames * window[:, None]).astype(jnp.bfloat16)
-    product_idx = sample_pos[:, None] * sample_pos[None, :] % channels
-    angles = 2.0 * math.pi * product_idx.astype(jnp.float32) / channels
-    dft_table = jnp.concatenate([jnp.cos(angles), -jnp.sin(angles)], axis=0).astype(jnp.bfloat16)
+    dft_table = jnp.asarray(first_table(channels))
     raw = jnp.dot(dft_table, windowed, preferred_element_type=jnp.float32)
     real_raw = raw[:channels]
     imag_raw = raw[channels:]
@@ -47,19 +46,26 @@
     return jnp.stack([real_out, imag_out]).astype(jnp.bfloat16)
 
 
+def table_angles(length):
+    positions = np.arange(length, dtype=np.int64)
+    product_idx = (positions[:, None] * positions[None, :] % length).astype(np.float32)
+    return (np.float32(2.0 * math.pi) * product_idx / np.float32(length)).astype(np.float64)
+
+
+def first_table(channels):
+    angles = table_angles(channels)
+    cosine = np.cos(angles).astype(np.float32)
+    sine = np.sin(angles).astype(np.float32)
+    return np.concatenate([cosine, -sine], axis=0).astype(jnp.bfloat16)
+
+
 def second_table(length):
-    positions = jnp.arange(length, dtype=jnp.int32)
-    angles = (
-        2.0
-        * math.pi
-        * (positions[:, None] * positions[None, :] % length).astype(jnp.float32)
-        / length
-    )
-    cosine = jnp.cos(angles) / math.sqrt(length)
-    sine = jnp.sin(angles) / math.sqrt(length)
-    upper = jnp.stack([cosine, -sine], axis=1)
-    lower = jnp.stack([sine, cosine], axis=1)
-    return jnp.stack([upper, lower]).astype(jnp.bfloat16)
+    angles = table_angles(length)
+    cosine = np.cos(angles).astype(np.float32) / np.float32(math.sqrt(length))
+    sine = np.sin(angles).astype(np.float32) / np.float32(math.sqrt(length))
+    upper = np.stack([cosine, -sine], axis=1)
+    lower = np.stack([sine, cosine], axis=1)
+    return jnp.asarray(np.stack([upper, lower]).astype(jnp.bfloat16))
 
 
 def pair_products(own_block, partner_block):

time: 71.1 us -> 70.4 us (level)
  blocking collectives: 0 us -> 32.2 us
  waiting for transfers between devices: 23.4 us -> 7.6 us
  starting transfers between devices: 34.7 us -> 19.9 us
  other arithmetic: 6.05 us -> 3.57 us
    all_to_all x0 -> x1, blocking collectives: none -> 32.2 us  [body(): lax.all_to_all(spectra, 'tm', split_axis=1, concat_axis=2, tiled=True)]
    all_to_all x1 -> x0, waiting for transfers between devices: 15.1 us -> none  [body(): lax.all_to_all(spectra, 'tm', split_axis=1, concat_axis=2, tiled=True)]
    all_to_all x1 -> x0, starting transfers between devices: 14.8 us -> none  [body(): lax.all_to_all(spectra, 'tm', split_axis=1, concat_axis=2, tiled=True)]
    another operation x8 -> x4, other arithmetic: 5.76 us -> 2.52 us
    ppermute x4, waiting for transfers between devices: 8.28 us -> 6.85 us  [passed_along(): lax.ppermute(value, axis, [(i, (i + by) % length) for i in range(length)])]
    unnamed x16 -> x4, local copies, waits for them, and re-layouts: 0.15 us -> 0.93 us
    concatenate x1, other arithmetic: 0.09 us -> 0.85 us  [body(): stream = jnp.concatenate([samples, tail_rim], axis=1).reshape(-1)]
    ppermute x1, waiting for transfers between devices: 0.01 us -> 0.75 us  [body(): tail_rim = lax.ppermute(head_rim, ('tm', 'seg'), pairs)]
  transfers between devices with their start and end apart: 6 -> 5, of which waited for: 2 -> 4; matrix products, arithmetic and copies ran while one was open for 7% -> 2% of each run, Pallas kernels for 0% -> 0%
where the time goes in v2:
time: 70.4 us; the launch traced here: 70 us
  blocking collectives  32.2 us (46%)
  starting transfers between devices  19.9 us (28%)
  waiting for transfers between devices  7.6 us (11%)
  local copies, waits for them, and re-layouts  4.28 us (6%)
  other arithmetic  3.57 us (5%)
  matrix products  2.2 us (3%)
    all_to_all x1, blocking collectives, body(): lax.all_to_all(spectra, 'tm', split_axis=1, concat_axis=2, tiled=True)  32.2 us
    ppermute x4, starting transfers between devices, passed_along(): lax.ppermute(value, axis, [(i, (i + by) % length) for i in range(length)])  11.1 us
    ppermute x1, starting transfers between devices, body(): tail_rim = lax.ppermute(head_rim, ('tm', 'seg'), pairs)  8.73 us
    ppermute x4, waiting for transfers between devices, passed_along(): lax.ppermute(value, axis, [(i, (i + by) % length) for i in range(length)])  6.85 us
    another operation x4, other arithmetic  2.52 us
    broadcast_in_dim x1, local copies, waits for them, and re-layouts, body(): return jnp.stack(results, axis=1)[None]  2.05 us
    dot_general x8, matrix products, transform(): jnp.einsum('ckbj,cjof->kbof', shaped, dft_table, preferred_element_type=j...  1.9 us
  transfers between devices with their start and end apart: 5, of which 4 were waited for; matrix products, arithmetic and copies ran while one was open for 2% of the time, Pallas kernels for 0%

profile of v2, /device:TPU:1, one launch (start us, length us, event | category | flops | bytes accessed | tf_op | source)
XLA Modules:
  0.0 70.0 jit_solution(4047168860428704038)
XLA Ops:
  0.0 0.7 slice.106
  0.7 8.7 %collective-permute-start = (f32[1,192]{1,0:T(1,128)S(1)}, f32[1,192]{1,0:T(1,128)S(1)}, u32[]{:S(2)}, u32[]{:S(2)}) collective-permute-start(f32[1,192]{1,0:T(1,128)S(1)} %slice.106), channel_id=1, source_target_pairs={{4,0},{8,4},{12,8},{16,12},{20,16},{24,20},{28,24},{32,28},{36,32}... | collective-permute-start | bytes 2312 | tf_op jit(solution)/shard_map/ppermute | solution.py:100
  9.5 0.8 %collective-permute-done = f32[1,192]{1,0:T(1,128)S(1)} collective-permute-done((f32[1,192]{1,0:T(1,128)S(1)}, f32[1,192]{1,0:T(1,128)S(1)}, u32[]{:S(2)}, u32[]{:S(2)}) %collective-permute-start) | collective-permute-done | bytes 800 | tf_op jit(solution)/shard_map/ppermute | solution.py:100
  10.2 0.8 %maximum_reduce_fusion = f32[8384]{0:T(1024)S(1)} fusion(f32[1,192]{1,0:T(1,128)S(1)} %collective-permute-done, f32[1,8192]{1,0:T(1,128)} %param.3), kind=kLoop, calls=%fused_computation.157 | loop fusion | flops 8384 | bytes 67072 | tf_op jit(solution)/shard_map/concatenate | solution.py:101
  11.2 0.9 %copy-done.1 = bf16[512,256]{1,0:T(8,128)(2,1)S(1)} copy-done((bf16[512,256]{1,0:T(8,128)(2,1)S(1)}, bf16[512,256]{1,0:T(8,128)(2,1)}, u32[]{:S(2)}) %copy-start.1) | copy-done | bytes 262168
  12.1 0.3 fusion.75
  12.7 32.2 %all_to_all.18 = bf16[2,256,128]{2,0,1:T(2,128)(2,1)S(1)} all-to-all(bf16[2,256,128]{2,0,1:T(2,128)(2,1)S(1)} %copy.10), channel_id=1, replica_groups=mesh['tm'=128,'seg'=4] {'tm'}, dimensions={1} | all-to-all | bytes 262144 | tf_op jit(solution)/shard_map/all_to_all | solution.py:104
  45.1 4.2 %collective-permute-start.3 = (bf16[2,2,16384]{2,1,0:T(2,128)(2,1)S(1)}, bf16[2,2,16384]{2,1,0:T(2,128)(2,1)S(1)}, u32[]{:S(2)}, u32[]{:S(2)}) collective-permute-start(bf16[2,2,16384]{2,1,0:T(2,128)(2,1)S(1)} %all_to_all.16), channel_id=1, source_target_pairs={{0,500},{4,504},{8,508},{12,0},{16,4},{20,8},{24,12},{28,16},{32,2... | collective-permute-start | bytes 393224 | tf_op jit(solution)/shard_map/ppermute | solution.py:16
  49.3 2.8 %collective-permute-start.2 = (bf16[2,2,16384]{2,1,0:T(2,128)(2,1)S(1)}, bf16[2,2,16384]{2,1,0:T(2,128)(2,1)S(1)}, u32[]{:S(2)}, u32[]{:S(2)}) collective-permute-start(bf16[2,2,16384]{2,1,0:T(2,128)(2,1)S(1)} %all_to_all.16), channel_id=1, source_target_pairs={{0,504},{4,508},{8,0},{12,4},{16,8},{20,12},{24,16},{28,20},{32,24... | collective-permute-start | bytes 393224 | tf_op jit(solution)/shard_map/ppermute | solution.py:16
  52.1 1.9 %collective-permute-start.1 = (bf16[2,2,16384]{2,1,0:T(2,128)(2,1)S(1)}, bf16[2,2,16384]{2,1,0:T(2,128)(2,1)S(1)}, u32[]{:S(2)}, u32[]{:S(2)}) collective-permute-start(bf16[2,2,16384]{2,1,0:T(2,128)(2,1)S(1)} %all_to_all.16), channel_id=1, source_target_pairs={{0,508},{4,0},{8,4},{12,8},{16,12},{20,16},{24,20},{28,24},{32,28}... | collective-permute-start | bytes 393224 | tf_op jit(solution)/shard_map/ppermute | solution.py:16
  54.2 2.2 %collective-permute-start.4 = (bf16[2,1,16384]{2,1,0:T(2,128)(2,1)S(1)}, bf16[2,1,16384]{2,1,0:T(2,128)(2,1)S(1)}, u32[]{:S(2)}, u32[]{:S(2)}) collective-permute-start(bf16[2,1,16384]{2,1,0:T(2,128)(2,1)S(1)} %bitcast.264), channel_id=1, source_target_pairs={{0,496},{4,500},{8,504},{12,508},{16,0},{20,4},{24,8},{28,12},{32,... | collective-permute-start | bytes 196616 | tf_op jit(solution)/shard_map/ppermute | solution.py:16
  56.7 1.4 %collective-permute-done.2 = bf16[2,2,16384]{2,1,0:T(2,128)(2,1)S(1)} collective-permute-done((bf16[2,2,16384]{2,1,0:T(2,128)(2,1)S(1)}, bf16[2,2,16384]{2,1,0:T(2,128)(2,1)S(1)}, u32[]{:S(2)}, u32[]{:S(2)}) %collective-permute-start.2) | collective-permute-done | bytes 131104 | tf_op jit(solution)/shard_map/ppermute | solution.py:16
  58.1 3.2 %collective-permute-done.1 = bf16[2,2,16384]{2,1,0:T(2,128)(2,1)S(1)} collective-permute-done((bf16[2,2,16384]{2,1,0:T(2,128)(2,1)S(1)}, bf16[2,2,16384]{2,1,0:T(2,128)(2,1)S(1)}, u32[]{:S(2)}, u32[]{:S(2)}) %collective-permute-start.1) | collective-permute-done | bytes 131104 | tf_op jit(solution)/shard_map/ppermute | solution.py:16
  61.3 0.9 %fusion.33 = (bf16[1,2,16384]{2,1,0:T(2,128)(2,1)S(1)}, bf16[1,2,16384]{2,1,0:T(2,128)(2,1)S(1)}, bf16[1,2,16384]{2,1,0:T(2,128)(2,1)S(1)}, bf16[1,2,16384]{2,1,...) fusion(f32[1,2,16384]{2,1,0:T(2,128)S(1)} %reshape.153, ...), kind=kLoop, calls=%fused_computation.72 | loop fusion | flops 1245184 | bytes 1310720 | tf_op jit(solution)/shard_map/convert.21
  62.2 2.2 %collective-permute-done.4 = bf16[2,1,16384]{2,1,0:T(2,128)(2,1)S(1)} collective-permute-done((bf16[2,1,16384]{2,1,0:T(2,128)(2,1)S(1)}, bf16[2,1,16384]{2,1,0:T(2,128)(2,1)S(1)}, u32[]{:S(2)}, u32[]{:S(2)}) %collective-permute-start.4) | collective-permute-done | bytes 65568 | tf_op jit(solution)/shard_map/ppermute | solution.py:16
  64.5 1.1 %fusion.49 = (bf16[1,2,16384]{2,1,0:T(2,128)(2,1)S(1)}, bf16[1,2,16384]{2,1,0:T(2,128)(2,1)S(1)}, bf16[1,2,16384]{2,1,0:T(2,128)(2,1)S(1)}, bf16[1,2,16384]{2,1,...) fusion(f32[1,2,16384]{2,1,0:T(2,128)S(1)} %reshape.153, ...), kind=kLoop, calls=%fused_computation.88 | loop fusion | flops 1572864 | bytes 1572864 | tf_op jit(solution)/shard_map/convert.5
  65.6 0.4 fusion.51
  66.2 0.2 fusion.21
  66.7 0.2 fusion.17
  67.0 0.2 fusion.15
  67.2 0.2 fusion.13
  67.4 0.2 fusion.11
  67.7 0.2 fusion.9
  67.9 2.1 %copy.12 = bf16[1,2,8,64,2,256]{5,4,3,2,1,0:T(2,128)(2,1)} copy(bf16[1,2,8,64,2,256]{5,3,4,1,2,0:T(8,128)(2,1)S(1)} %bitcast.263) | data formatting | bytes 2097152 | tf_op jit(solution)/shard_map/broadcast_in_dim | solution.py:122
  (27 shorter events, 1.3 us)
Async XLA Ops:
  0.7 9.5 %collective-permute-start = (f32[1,192]{1,0:T(1,128)S(1)}, f32[1,192]{1,0:T(1,128)S(1)}, u32[]{:S(2)}, u32[]{:S(2)}) collective-permute-start(f32[1,192]{1,0:T(1,128)S(1)} %slice.106), channel_id=1, source_target_pairs={{4,0},{8,4},{12,8},{16,12},{20,16},{24,20},{28,24},{32,28},{36,32}... | collective-permute-start | bytes 2312 | tf_op jit(solution)/shard_map/ppermute | solution.py:100
  11.2 1.0 %copy-start.1 = (bf16[512,256]{1,0:T(8,128)(2,1)S(1)}, bf16[512,256]{1,0:T(8,128)(2,1)}, u32[]{:S(2)}) copy-start(bf16[512,256]{1,0:T(8,128)(2,1)} %constant.34.clone) | copy-start | bytes 786436
  45.0 11.4 %copy-start = (bf16[2,256,2,256,1]{3,1,0,2,4:T(8,128)(2,1)S(1)}, bf16[2,256,2,256,1]{3,1,0,2,4:T(8,128)(2,1)}, u32[]{:S(2)}) copy-start(bf16[2,256,2,256,1]{3,1,0,2,4:T(8,128)(2,1)} %constant.37) | copy-start | bytes 1572868
  45.1 19.4 %collective-permute-start.3 = (bf16[2,2,16384]{2,1,0:T(2,128)(2,1)S(1)}, bf16[2,2,16384]{2,1,0:T(2,128)(2,1)S(1)}, u32[]{:S(2)}, u32[]{:S(2)}) collective-permute-start(bf16[2,2,16384]{2,1,0:T(2,128)(2,1)S(1)} %all_to_all.16), channel_id=1, source_target_pairs={{0,500},{4,504},{8,508},{12,0},{16,4},{20,8},{24,12},{28,16},{32,2... | collective-permute-start | bytes 393224 | tf_op jit(solution)/shard_map/ppermute | solution.py:16
  49.3 8.8 %collective-permute-start.2 = (bf16[2,2,16384]{2,1,0:T(2,128)(2,1)S(1)}, bf16[2,2,16384]{2,1,0:T(2,128)(2,1)S(1)}, u32[]{:S(2)}, u32[]{:S(2)}) collective-permute-start(bf16[2,2,16384]{2,1,0:T(2,128)(2,1)S(1)} %all_to_all.16), channel_id=1, source_target_pairs={{0,504},{4,508},{8,0},{12,4},{16,8},{20,12},{24,16},{28,20},{32,24... | collective-permute-start | bytes 393224 | tf_op jit(solution)/shard_map/ppermute | solution.py:16
  52.1 9.2 %collective-permute-start.1 = (bf16[2,2,16384]{2,1,0:T(2,128)(2,1)S(1)}, bf16[2,2,16384]{2,1,0:T(2,128)(2,1)S(1)}, u32[]{:S(2)}, u32[]{:S(2)}) collective-permute-start(bf16[2,2,16384]{2,1,0:T(2,128)(2,1)S(1)} %all_to_all.16), channel_id=1, source_target_pairs={{0,508},{4,0},{8,4},{12,8},{16,12},{20,16},{24,20},{28,24},{32,28}... | collective-permute-start | bytes 393224 | tf_op jit(solution)/shard_map/ppermute | solution.py:16
  54.2 10.3 %collective-permute-start.4 = (bf16[2,1,16384]{2,1,0:T(2,128)(2,1)S(1)}, bf16[2,1,16384]{2,1,0:T(2,128)(2,1)S(1)}, u32[]{:S(2)}, u32[]{:S(2)}) collective-permute-start(bf16[2,1,16384]{2,1,0:T(2,128)(2,1)S(1)} %bitcast.264), channel_id=1, source_target_pairs={{0,496},{4,500},{8,504},{12,508},{16,0},{20,4},{24,8},{28,12},{32,... | collective-permute-start | bytes 196616 | tf_op jit(solution)/shard_map/ppermute | solution.py:16

commit v3 on v2

--- a/solution.py
+++ b/solution.py
@@ -16,7 +16,7 @@
     return lax.ppermute(value, axis, [(i, (i + by) % length) for i in range(length)])
 
 
-def channelize(stream, frame_count, channels):
+def channelize(stream, frame_count, channels, dft_table):
     hop_len = channels // 4
     rows = stream.reshape(frame_count + 3, hop_len).T
     frames = jnp.concatenate(
@@ -27,7 +27,6 @@
         0.5 - 0.5 * jnp.cos(2.0 * math.pi * sample_pos.astype(jnp.float32) / channels)
     ) / math.sqrt(3.0 * channels / 8.0)
     windowed = (frames * window[:, None]).astype(jnp.bfloat16)
-    dft_table = jnp.asarray(first_table(channels))
     raw = jnp.dot(dft_table, windowed, preferred_element_type=jnp.float32)
     real_raw = raw[:channels]
     imag_raw = raw[channels:]
@@ -92,6 +91,8 @@
     hop_len = NP // 4
     frame_count = samples.shape[1] // hop_len
     head_rim = samples[:, : 3 * hop_len]
+    unit = (samples[0, 0] * 0.0 + 1.0).astype(jnp.bfloat16)
+    dft_table = lax.optimization_barrier(jnp.asarray(first_table(NP)) * unit)
     def flat(s, t):
         return t * seg_count + s
 
@@ -99,7 +100,7 @@
     pairs += [(flat(s + 1, 0), flat(s, tm_count - 1)) for s in range(seg_count - 1)]
     tail_rim = lax.ppermute(head_rim, ("tm", "seg"), pairs)
     stream = jnp.concatenate([samples, tail_rim], axis=1).reshape(-1)
-    spectra = channelize(stream, frame_count, NP)
+    spectra = channelize(stream, frame_count, NP, dft_table)
     per_dev = NP // tm_count
     gathered = lax.all_to_all(spectra, "tm", split_axis=1, concat_axis=2, tiled=True)
     pieces = [gathered]

time: 70.4 us -> 69.2 us (0.983)
  blocking collectives: 32.2 us -> 30.7 us
  waiting for transfers between devices: 7.6 us -> 6.85 us
    all_to_all x1, blocking collectives: 32.2 us -> 30.7 us  [body(): lax.all_to_all(spectra, 'tm', split_axis=1, concat_axis=2, tiled=True)]
    slice x0 -> x1, local copies, waits for them, and re-layouts: none -> 1.17 us  [body(): unit = (samples[0, 0] * 0.0 + 1.0).astype(jnp.bfloat16)]
    mul x0 -> x1, other arithmetic: none -> 0.98 us  [body(): dft_table = lax.optimization_barrier(jnp.asarray(first_table(NP)) * unit)]
    unnamed x4, local copies, waits for them, and re-layouts: 0.93 us -> 0.01 us
    concatenate x1, other arithmetic: 0.85 us -> 0.09 us  [body(): stream = jnp.concatenate([samples, tail_rim], axis=1).reshape(-1)]
    ppermute x1, waiting for transfers between devices: 0.75 us -> 0.01 us  [body(): tail_rim = lax.ppermute(head_rim, ('tm', 'seg'), pairs)]
  transfers between devices with their start and end apart: 5 -> 5, of which waited for: 4 -> 3; matrix products, arithmetic and copies ran while one was open for 2% -> 5% of each run, Pallas kernels for 0% -> 0%
where the time goes in v3:
time: 69.2 us; the launch traced here: 68.9 us
  blocking collectives  30.7 us (44%)
  starting transfers between devices  19.9 us (29%)
  waiting for transfers between devices  6.85 us (10%)
  local copies, waits for them, and re-layouts  4.53 us (7%)
  other arithmetic  3.78 us (5%)
  matrix products  2.2 us (3%)
  between operations  0.98 us (1%)
    all_to_all x1, blocking collectives, body(): lax.all_to_all(spectra, 'tm', split_axis=1, concat_axis=2, tiled=True)  30.7 us
    ppermute x4, starting transfers between devices, passed_along(): lax.ppermute(value, axis, [(i, (i + by) % length) for i in range(length)])  11.1 us
    ppermute x1, starting transfers between devices, body(): tail_rim = lax.ppermute(head_rim, ('tm', 'seg'), pairs)  8.73 us
    ppermute x4, waiting for transfers between devices, passed_along(): lax.ppermute(value, axis, [(i, (i + by) % length) for i in range(length)])  6.85 us
    another operation x4, other arithmetic  2.52 us
    broadcast_in_dim x1, local copies, waits for them, and re-layouts, body(): return jnp.stack(results, axis=1)[None]  2.05 us
    dot_general x8, matrix products, transform(): jnp.einsum('ckbj,cjof->kbof', shaped, dft_table, preferred_element_type=j...  1.9 us
  transfers between devices with their start and end apart: 5, of which 3 were waited for; matrix products, arithmetic and copies ran while one was open for 5% of the time, Pallas kernels for 0%

profile of v3, /device:TPU:1, one launch (start us, length us, event | category | flops | bytes accessed | tf_op | source)
XLA Modules:
  0.0 68.9 jit_solution(1487400479754771921)
XLA Ops:
  0.0 0.7 slice.110
  0.7 8.7 %collective-permute-start = (f32[1,192]{1,0:T(1,128)S(1)}, f32[1,192]{1,0:T(1,128)S(1)}, u32[]{:S(2)}, u32[]{:S(2)}) collective-permute-start(f32[1,192]{1,0:T(1,128)S(1)} %slice.110), channel_id=1, source_target_pairs={{4,0},{8,4},{12,8},{16,12},{20,16},{24,20},{28,24},{32,28},{36,32}... | collective-permute-start | bytes 2312 | tf_op jit(solution)/shard_map/ppermute | solution.py:101
  9.4 1.2 %slice.109 = f32[1,1]{1,0:T(1,128)} slice(f32[1,8192]{1,0:T(1,128)} %param.3), slice={[0:1], [0:1]} | slice | bytes 8 | tf_op jit(solution)/shard_map/slice | solution.py:94
  11.3 1.0 %broadcast_multiply_fusion = bf16[512,256]{1,0:T(8,128)(2,1)S(1)} fusion(bf16[512,256]{1,0:T(8,128)(2,1)} %constant.40.clone, bf16[]{:T(256)} %bitcast), kind=kLoop, calls=%fused_computation.124 | loop fusion | flops 131072 | bytes 524290 | tf_op jit(solution)/shard_map/mul | solution.py:95
  12.5 0.3 fusion.75
  13.1 30.7 %all_to_all.18 = bf16[2,256,128]{2,0,1:T(2,128)(2,1)S(1)} all-to-all(bf16[2,256,128]{2,0,1:T(2,128)(2,1)S(1)} %copy.10), channel_id=1, replica_groups=mesh['tm'=128,'seg'=4] {'tm'}, dimensions={1} | all-to-all | bytes 262144 | tf_op jit(solution)/shard_map/all_to_all | solution.py:105
  44.0 4.2 %collective-permute-start.3 = (bf16[2,2,16384]{2,1,0:T(2,128)(2,1)S(1)}, bf16[2,2,16384]{2,1,0:T(2,128)(2,1)S(1)}, u32[]{:S(2)}, u32[]{:S(2)}) collective-permute-start(bf16[2,2,16384]{2,1,0:T(2,128)(2,1)S(1)} %all_to_all.16), channel_id=1, source_target_pairs={{0,500},{4,504},{8,508},{12,0},{16,4},{20,8},{24,12},{28,16},{32,2... | collective-permute-start | bytes 393224 | tf_op jit(solution)/shard_map/ppermute | solution.py:16
  48.2 2.8 %collective-permute-start.2 = (bf16[2,2,16384]{2,1,0:T(2,128)(2,1)S(1)}, bf16[2,2,16384]{2,1,0:T(2,128)(2,1)S(1)}, u32[]{:S(2)}, u32[]{:S(2)}) collective-permute-start(bf16[2,2,16384]{2,1,0:T(2,128)(2,1)S(1)} %all_to_all.16), channel_id=1, source_target_pairs={{0,504},{4,508},{8,0},{12,4},{16,8},{20,12},{24,16},{28,20},{32,24... | collective-permute-start | bytes 393224 | tf_op jit(solution)/shard_map/ppermute | solution.py:16
  51.0 1.9 %collective-permute-start.1 = (bf16[2,2,16384]{2,1,0:T(2,128)(2,1)S(1)}, bf16[2,2,16384]{2,1,0:T(2,128)(2,1)S(1)}, u32[]{:S(2)}, u32[]{:S(2)}) collective-permute-start(bf16[2,2,16384]{2,1,0:T(2,128)(2,1)S(1)} %all_to_all.16), channel_id=1, source_target_pairs={{0,508},{4,0},{8,4},{12,8},{16,12},{20,16},{24,20},{28,24},{32,28}... | collective-permute-start | bytes 393224 | tf_op jit(solution)/shard_map/ppermute | solution.py:16
  53.1 2.2 %collective-permute-start.4 = (bf16[2,1,16384]{2,1,0:T(2,128)(2,1)S(1)}, bf16[2,1,16384]{2,1,0:T(2,128)(2,1)S(1)}, u32[]{:S(2)}, u32[]{:S(2)}) collective-permute-start(bf16[2,1,16384]{2,1,0:T(2,128)(2,1)S(1)} %bitcast.265), channel_id=1, source_target_pairs={{0,496},{4,500},{8,504},{12,508},{16,0},{20,4},{24,8},{28,12},{32,... | collective-permute-start | bytes 196616 | tf_op jit(solution)/shard_map/ppermute | solution.py:16
  55.6 1.4 %collective-permute-done.2 = bf16[2,2,16384]{2,1,0:T(2,128)(2,1)S(1)} collective-permute-done((bf16[2,2,16384]{2,1,0:T(2,128)(2,1)S(1)}, bf16[2,2,16384]{2,1,0:T(2,128)(2,1)S(1)}, u32[]{:S(2)}, u32[]{:S(2)}) %collective-permute-start.2) | collective-permute-done | bytes 131104 | tf_op jit(solution)/shard_map/ppermute | solution.py:16
  57.0 3.2 %collective-permute-done.1 = bf16[2,2,16384]{2,1,0:T(2,128)(2,1)S(1)} collective-permute-done((bf16[2,2,16384]{2,1,0:T(2,128)(2,1)S(1)}, bf16[2,2,16384]{2,1,0:T(2,128)(2,1)S(1)}, u32[]{:S(2)}, u32[]{:S(2)}) %collective-permute-start.1) | collective-permute-done | bytes 131104 | tf_op jit(solution)/shard_map/ppermute | solution.py:16
  60.2 0.9 %fusion.33 = (bf16[1,2,16384]{2,1,0:T(2,128)(2,1)S(1)}, bf16[1,2,16384]{2,1,0:T(2,128)(2,1)S(1)}, bf16[1,2,16384]{2,1,0:T(2,128)(2,1)S(1)}, bf16[1,2,16384]{2,1,...) fusion(f32[1,2,16384]{2,1,0:T(2,128)S(1)} %reshape.158, ...), kind=kLoop, calls=%fused_computation.72 | loop fusion | flops 1245184 | bytes 1310720 | tf_op jit(solution)/shard_map/convert.21
  61.2 2.2 %collective-permute-done.4 = bf16[2,1,16384]{2,1,0:T(2,128)(2,1)S(1)} collective-permute-done((bf16[2,1,16384]{2,1,0:T(2,128)(2,1)S(1)}, bf16[2,1,16384]{2,1,0:T(2,128)(2,1)S(1)}, u32[]{:S(2)}, u32[]{:S(2)}) %collective-permute-start.4) | collective-permute-done | bytes 65568 | tf_op jit(solution)/shard_map/ppermute | solution.py:16
  63.4 1.1 %fusion.49 = (bf16[1,2,16384]{2,1,0:T(2,128)(2,1)S(1)}, bf16[1,2,16384]{2,1,0:T(2,128)(2,1)S(1)}, bf16[1,2,16384]{2,1,0:T(2,128)(2,1)S(1)}, bf16[1,2,16384]{2,1,...) fusion(f32[1,2,16384]{2,1,0:T(2,128)S(1)} %reshape.158, ...), kind=kLoop, calls=%fused_computation.88 | loop fusion | flops 1572864 | bytes 1572864 | tf_op jit(solution)/shard_map/convert.5
  64.6 0.4 fusion.51
  65.1 0.2 fusion.21
  65.4 0.2 fusion.19
  65.6 0.2 fusion.17
  65.9 0.2 fusion.15
  66.1 0.2 fusion.13
  66.4 0.2 fusion.11
  66.6 0.2 fusion.9
  66.8 2.1 %copy.12 = bf16[1,2,8,64,2,256]{5,4,3,2,1,0:T(2,128)(2,1)} copy(bf16[1,2,8,64,2,256]{5,3,4,1,2,0:T(8,128)(2,1)S(1)} %bitcast.264) | data formatting | bytes 2097152 | tf_op jit(solution)/shard_map/broadcast_in_dim | solution.py:123
  (29 shorter events, 1.2 us)
Async XLA Ops:
  0.7 11.6 %collective-permute-start = (f32[1,192]{1,0:T(1,128)S(1)}, f32[1,192]{1,0:T(1,128)S(1)}, u32[]{:S(2)}, u32[]{:S(2)}) collective-permute-start(f32[1,192]{1,0:T(1,128)S(1)} %slice.110), channel_id=1, source_target_pairs={{4,0},{8,4},{12,8},{16,12},{20,16},{24,20},{28,24},{32,28},{36,32}... | collective-permute-start | bytes 2312 | tf_op jit(solution)/shard_map/ppermute | solution.py:101
  11.2 1.0 %copy-start.1 = (f32[1,8192]{1,0:T(1,128)S(1)}, f32[1,8192]{1,0:T(1,128)}, u32[]{:S(2)}) copy-start(f32[1,8192]{1,0:T(1,128)} %param.3) | copy-start | bytes 98308
  43.9 11.4 %copy-start = (bf16[2,256,2,256,1]{3,1,0,2,4:T(8,128)(2,1)S(1)}, bf16[2,256,2,256,1]{3,1,0,2,4:T(8,128)(2,1)}, u32[]{:S(2)}) copy-start(bf16[2,256,2,256,1]{3,1,0,2,4:T(8,128)(2,1)} %constant.43) | copy-start | bytes 1572868
  44.0 19.4 %collective-permute-start.3 = (bf16[2,2,16384]{2,1,0:T(2,128)(2,1)S(1)}, bf16[2,2,16384]{2,1,0:T(2,128)(2,1)S(1)}, u32[]{:S(2)}, u32[]{:S(2)}) collective-permute-start(bf16[2,2,16384]{2,1,0:T(2,128)(2,1)S(1)} %all_to_all.16), channel_id=1, source_target_pairs={{0,500},{4,504},{8,508},{12,0},{16,4},{20,8},{24,12},{28,16},{32,2... | collective-permute-start | bytes 393224 | tf_op jit(solution)/shard_map/ppermute | solution.py:16
  48.2 8.8 %collective-permute-start.2 = (bf16[2,2,16384]{2,1,0:T(2,128)(2,1)S(1)}, bf16[2,2,16384]{2,1,0:T(2,128)(2,1)S(1)}, u32[]{:S(2)}, u32[]{:S(2)}) collective-permute-start(bf16[2,2,16384]{2,1,0:T(2,128)(2,1)S(1)} %all_to_all.16), channel_id=1, source_target_pairs={{0,504},{4,508},{8,0},{12,4},{16,8},{20,12},{24,16},{28,20},{32,24... | collective-permute-start | bytes 393224 | tf_op jit(solution)/shard_map/ppermute | solution.py:16
  51.0 9.2 %collective-permute-start.1 = (bf16[2,2,16384]{2,1,0:T(2,128)(2,1)S(1)}, bf16[2,2,16384]{2,1,0:T(2,128)(2,1)S(1)}, u32[]{:S(2)}, u32[]{:S(2)}) collective-permute-start(bf16[2,2,16384]{2,1,0:T(2,128)(2,1)S(1)} %all_to_all.16), channel_id=1, source_target_pairs={{0,508},{4,0},{8,4},{12,8},{16,12},{20,16},{24,20},{28,24},{32,28}... | collective-permute-start | bytes 393224 | tf_op jit(solution)/shard_map/ppermute | solution.py:16
  53.1 10.3 %collective-permute-start.4 = (bf16[2,1,16384]{2,1,0:T(2,128)(2,1)S(1)}, bf16[2,1,16384]{2,1,0:T(2,128)(2,1)S(1)}, u32[]{:S(2)}, u32[]{:S(2)}) collective-permute-start(bf16[2,1,16384]{2,1,0:T(2,128)(2,1)S(1)} %bitcast.265), channel_id=1, source_target_pairs={{0,496},{4,500},{8,504},{12,508},{16,0},{20,4},{24,8},{28,12},{32,... | collective-permute-start | bytes 196616 | tf_op jit(solution)/shard_map/ppermute | solution.py:16

commit v4 on v3

--- a/solution.py
+++ b/solution.py
@@ -91,7 +91,7 @@
     hop_len = NP // 4
     frame_count = samples.shape[1] // hop_len
     head_rim = samples[:, : 3 * hop_len]
-    unit = (samples[0, 0] * 0.0 + 1.0).astype(jnp.bfloat16)
+    unit = (lax.axis_index("tm") >= 0).astype(jnp.bfloat16)
     dft_table = lax.optimization_barrier(jnp.asarray(first_table(NP)) * unit)
     def flat(s, t):
         return t * seg_count + s

time: 69.2 us -> 68.6 us (level)
  blocking collectives: 30.7 us -> 31.9 us
  local copies, waits for them, and re-layouts: 4.53 us -> 3.36 us
    all_to_all x1, blocking collectives: 30.7 us -> 31.9 us  [body(): lax.all_to_all(spectra, 'tm', split_axis=1, concat_axis=2, tiled=True)]
    slice x1 -> x0, local copies, waits for them, and re-layouts: 1.17 us -> none  [body(): unit = (samples[0, 0] * 0.0 + 1.0).astype(jnp.bfloat16)]
  transfers between devices with their start and end apart: 5 -> 5, of which waited for: 3 -> 3; matrix products, arithmetic and copies ran while one was open for 5% -> 4% of each run, Pallas kernels for 0% -> 0%
where the time goes in v4:
time: 68.6 us; the launch traced here: 68.3 us
  blocking collectives  31.9 us (47%)
  starting transfers between devices  19.9 us (29%)
  waiting for transfers between devices  6.85 us (10%)
  other arithmetic  3.78 us (6%)
  local copies, waits for them, and re-layouts  3.36 us (5%)
  matrix products  2.2 us (3%)
    all_to_all x1, blocking collectives, body(): lax.all_to_all(spectra, 'tm', split_axis=1, concat_axis=2, tiled=True)  31.9 us
    ppermute x4, starting transfers between devices, passed_along(): lax.ppermute(value, axis, [(i, (i + by) % length) for i in range(length)])  11.1 us
    ppermute x1, starting transfers between devices, body(): tail_rim = lax.ppermute(head_rim, ('tm', 'seg'), pairs)  8.73 us
    ppermute x4, waiting for transfers between devices, passed_along(): lax.ppermute(value, axis, [(i, (i + by) % length) for i in range(length)])  6.85 us
    another operation x4, other arithmetic  2.52 us
    broadcast_in_dim x1, local copies, waits for them, and re-layouts, body(): return jnp.stack(results, axis=1)[None]  2.06 us
    dot_general x8, matrix products, transform(): jnp.einsum('ckbj,cjof->kbof', shaped, dft_table, preferred_element_type=j...  1.9 us
  transfers between devices with their start and end apart: 5, of which 3 were waited for; matrix products, arithmetic and copies ran while one was open for 4% of the time, Pallas kernels for 0%

profile of v4, /device:TPU:1, one launch (start us, length us, event | category | flops | bytes accessed | tf_op | source)
XLA Modules:
  0.0 68.3 jit_solution(9864918967309080833)
XLA Ops:
  0.0 0.7 slice.106
  0.7 8.7 %collective-permute-start = (f32[1,192]{1,0:T(1,128)S(1)}, f32[1,192]{1,0:T(1,128)S(1)}, u32[]{:S(2)}, u32[]{:S(2)}) collective-permute-start(f32[1,192]{1,0:T(1,128)S(1)} %slice.106), channel_id=1, source_target_pairs={{4,0},{8,4},{12,8},{16,12},{20,16},{24,20},{28,24},{32,28},{36,32}... | collective-permute-start | bytes 2312 | tf_op jit(solution)/shard_map/ppermute | solution.py:101
  9.4 1.0 %broadcast_multiply_fusion = bf16[512,256]{1,0:T(8,128)(2,1)S(1)} fusion(bf16[512,256]{1,0:T(8,128)(2,1)} %constant.41.clone, bf16[]{:T(256)S(6)} %convert_element_type.222), kind=kLoop, calls=%fused_computation.124 | loop fusion | flops 131072 | bytes 524290 | tf_op jit(solution)/shard_map/mul | solution.py:95
  10.7 0.3 fusion.75
  11.3 31.9 %all_to_all.18 = bf16[2,256,128]{2,0,1:T(2,128)(2,1)S(1)} all-to-all(bf16[2,256,128]{2,0,1:T(2,128)(2,1)S(1)} %copy.10), channel_id=1, replica_groups=mesh['tm'=128,'seg'=4] {'tm'}, dimensions={1} | all-to-all | bytes 262144 | tf_op jit(solution)/shard_map/all_to_all | solution.py:105
  43.4 4.2 %collective-permute-start.3 = (bf16[2,2,16384]{2,1,0:T(2,128)(2,1)S(1)}, bf16[2,2,16384]{2,1,0:T(2,128)(2,1)S(1)}, u32[]{:S(2)}, u32[]{:S(2)}) collective-permute-start(bf16[2,2,16384]{2,1,0:T(2,128)(2,1)S(1)} %all_to_all.16), channel_id=1, source_target_pairs={{0,500},{4,504},{8,508},{12,0},{16,4},{20,8},{24,12},{28,16},{32,2... | collective-permute-start | bytes 393224 | tf_op jit(solution)/shard_map/ppermute | solution.py:16
  47.6 2.8 %collective-permute-start.2 = (bf16[2,2,16384]{2,1,0:T(2,128)(2,1)S(1)}, bf16[2,2,16384]{2,1,0:T(2,128)(2,1)S(1)}, u32[]{:S(2)}, u32[]{:S(2)}) collective-permute-start(bf16[2,2,16384]{2,1,0:T(2,128)(2,1)S(1)} %all_to_all.16), channel_id=1, source_target_pairs={{0,504},{4,508},{8,0},{12,4},{16,8},{20,12},{24,16},{28,20},{32,24... | collective-permute-start | bytes 393224 | tf_op jit(solution)/shard_map/ppermute | solution.py:16
  50.4 1.9 %collective-permute-start.1 = (bf16[2,2,16384]{2,1,0:T(2,128)(2,1)S(1)}, bf16[2,2,16384]{2,1,0:T(2,128)(2,1)S(1)}, u32[]{:S(2)}, u32[]{:S(2)}) collective-permute-start(bf16[2,2,16384]{2,1,0:T(2,128)(2,1)S(1)} %all_to_all.16), channel_id=1, source_target_pairs={{0,508},{4,0},{8,4},{12,8},{16,12},{20,16},{24,20},{28,24},{32,28}... | collective-permute-start | bytes 393224 | tf_op jit(solution)/shard_map/ppermute | solution.py:16
  52.5 2.2 %collective-permute-start.4 = (bf16[2,1,16384]{2,1,0:T(2,128)(2,1)S(1)}, bf16[2,1,16384]{2,1,0:T(2,128)(2,1)S(1)}, u32[]{:S(2)}, u32[]{:S(2)}) collective-permute-start(bf16[2,1,16384]{2,1,0:T(2,128)(2,1)S(1)} %bitcast.264), channel_id=1, source_target_pairs={{0,496},{4,500},{8,504},{12,508},{16,0},{20,4},{24,8},{28,12},{32,... | collective-permute-start | bytes 196616 | tf_op jit(solution)/shard_map/ppermute | solution.py:16
  54.8 0.2 fusion.23
  55.0 1.4 %collective-permute-done.2 = bf16[2,2,16384]{2,1,0:T(2,128)(2,1)S(1)} collective-permute-done((bf16[2,2,16384]{2,1,0:T(2,128)(2,1)S(1)}, bf16[2,2,16384]{2,1,0:T(2,128)(2,1)S(1)}, u32[]{:S(2)}, u32[]{:S(2)}) %collective-permute-start.2) | collective-permute-done | bytes 131104 | tf_op jit(solution)/shard_map/ppermute | solution.py:16
  56.4 3.2 %collective-permute-done.1 = bf16[2,2,16384]{2,1,0:T(2,128)(2,1)S(1)} collective-permute-done((bf16[2,2,16384]{2,1,0:T(2,128)(2,1)S(1)}, bf16[2,2,16384]{2,1,0:T(2,128)(2,1)S(1)}, u32[]{:S(2)}, u32[]{:S(2)}) %collective-permute-start.1) | collective-permute-done | bytes 131104 | tf_op jit(solution)/shard_map/ppermute | solution.py:16
  59.6 0.9 %fusion.33 = (bf16[1,2,16384]{2,1,0:T(2,128)(2,1)S(1)}, bf16[1,2,16384]{2,1,0:T(2,128)(2,1)S(1)}, bf16[1,2,16384]{2,1,0:T(2,128)(2,1)S(1)}, bf16[1,2,16384]{2,1,...) fusion(f32[1,2,16384]{2,1,0:T(2,128)S(1)} %reshape.153, ...), kind=kLoop, calls=%fused_computation.72 | loop fusion | flops 1245184 | bytes 1310720 | tf_op jit(solution)/shard_map/convert.21
  60.6 2.2 %collective-permute-done.4 = bf16[2,1,16384]{2,1,0:T(2,128)(2,1)S(1)} collective-permute-done((bf16[2,1,16384]{2,1,0:T(2,128)(2,1)S(1)}, bf16[2,1,16384]{2,1,0:T(2,128)(2,1)S(1)}, u32[]{:S(2)}, u32[]{:S(2)}) %collective-permute-start.4) | collective-permute-done | bytes 65568 | tf_op jit(solution)/shard_map/ppermute | solution.py:16
  62.8 1.1 %fusion.49 = (bf16[1,2,16384]{2,1,0:T(2,128)(2,1)S(1)}, bf16[1,2,16384]{2,1,0:T(2,128)(2,1)S(1)}, bf16[1,2,16384]{2,1,0:T(2,128)(2,1)S(1)}, bf16[1,2,16384]{2,1,...) fusion(f32[1,2,16384]{2,1,0:T(2,128)S(1)} %reshape.153, ...), kind=kLoop, calls=%fused_computation.88 | loop fusion | flops 1572864 | bytes 1572864 | tf_op jit(solution)/shard_map/convert.5
  64.0 0.4 fusion.51
  64.5 0.2 fusion.21
  64.8 0.2 fusion.19
  65.0 0.2 fusion.17
  65.3 0.2 fusion.15
  65.5 0.2 fusion.13
  65.8 0.2 fusion.11
  66.0 0.2 fusion.9
  66.3 2.1 %copy.12 = bf16[1,2,8,64,2,256]{5,4,3,2,1,0:T(2,128)(2,1)} copy(bf16[1,2,8,64,2,256]{5,3,4,1,2,0:T(8,128)(2,1)S(1)} %bitcast.263) | data formatting | bytes 2097152 | tf_op jit(solution)/shard_map/broadcast_in_dim | solution.py:123
  (28 shorter events, 1.0 us)
Async XLA Ops:
  0.7 9.8 %collective-permute-start = (f32[1,192]{1,0:T(1,128)S(1)}, f32[1,192]{1,0:T(1,128)S(1)}, u32[]{:S(2)}, u32[]{:S(2)}) collective-permute-start(f32[1,192]{1,0:T(1,128)S(1)} %slice.106), channel_id=1, source_target_pairs={{4,0},{8,4},{12,8},{16,12},{20,16},{24,20},{28,24},{32,28},{36,32}... | collective-permute-start | bytes 2312 | tf_op jit(solution)/shard_map/ppermute | solution.py:101
  9.4 1.0 %copy-start.1 = (f32[1,8192]{1,0:T(1,128)S(1)}, f32[1,8192]{1,0:T(1,128)}, u32[]{:S(2)}) copy-start(f32[1,8192]{1,0:T(1,128)} %param.3) | copy-start | bytes 98308
  43.3 11.4 %copy-start = (bf16[2,256,2,256,1]{3,1,0,2,4:T(8,128)(2,1)S(1)}, bf16[2,256,2,256,1]{3,1,0,2,4:T(8,128)(2,1)}, u32[]{:S(2)}) copy-start(bf16[2,256,2,256,1]{3,1,0,2,4:T(8,128)(2,1)} %constant.44) | copy-start | bytes 1572868
  43.4 19.4 %collective-permute-start.3 = (bf16[2,2,16384]{2,1,0:T(2,128)(2,1)S(1)}, bf16[2,2,16384]{2,1,0:T(2,128)(2,1)S(1)}, u32[]{:S(2)}, u32[]{:S(2)}) collective-permute-start(bf16[2,2,16384]{2,1,0:T(2,128)(2,1)S(1)} %all_to_all.16), channel_id=1, source_target_pairs={{0,500},{4,504},{8,508},{12,0},{16,4},{20,8},{24,12},{28,16},{32,2... | collective-permute-start | bytes 393224 | tf_op jit(solution)/shard_map/ppermute | solution.py:16
  47.6 8.8 %collective-permute-start.2 = (bf16[2,2,16384]{2,1,0:T(2,128)(2,1)S(1)}, bf16[2,2,16384]{2,1,0:T(2,128)(2,1)S(1)}, u32[]{:S(2)}, u32[]{:S(2)}) collective-permute-start(bf16[2,2,16384]{2,1,0:T(2,128)(2,1)S(1)} %all_to_all.16), channel_id=1, source_target_pairs={{0,504},{4,508},{8,0},{12,4},{16,8},{20,12},{24,16},{28,20},{32,24... | collective-permute-start | bytes 393224 | tf_op jit(solution)/shard_map/ppermute | solution.py:16
  50.4 9.2 %collective-permute-start.1 = (bf16[2,2,16384]{2,1,0:T(2,128)(2,1)S(1)}, bf16[2,2,16384]{2,1,0:T(2,128)(2,1)S(1)}, u32[]{:S(2)}, u32[]{:S(2)}) collective-permute-start(bf16[2,2,16384]{2,1,0:T(2,128)(2,1)S(1)} %all_to_all.16), channel_id=1, source_target_pairs={{0,508},{4,0},{8,4},{12,8},{16,12},{20,16},{24,20},{28,24},{32,28}... | collective-permute-start | bytes 393224 | tf_op jit(solution)/shard_map/ppermute | solution.py:16
  52.5 10.3 %collective-permute-start.4 = (bf16[2,1,16384]{2,1,0:T(2,128)(2,1)S(1)}, bf16[2,1,16384]{2,1,0:T(2,128)(2,1)S(1)}, u32[]{:S(2)}, u32[]{:S(2)}) collective-permute-start(bf16[2,1,16384]{2,1,0:T(2,128)(2,1)S(1)} %bitcast.264), channel_id=1, source_target_pairs={{0,496},{4,500},{8,504},{12,508},{16,0},{20,4},{24,8},{28,12},{32,... | collective-permute-start | bytes 196616 | tf_op jit(solution)/shard_map/ppermute | solution.py:16
